TPU v7x, 128 devices: a whole 4x4x4 slice. The times are simulated.
128 devices in a mesh: wide: 16 (over z, y), col: 8 (over x, core).
Axes of the slice: x: 4, y: 4, z: 4, core: 2. Of those that a mesh axis runs over, the one named last changes fastest.
Arguments:
- z_root: float32 [512, 16384], P('col', 'wide'), may hold values from -6 to 6
- z_child: float32 [512, 2, 8192], P('col', None, 'wide'), may hold values from -6 to 6
- z_grand: float32 [512, 4, 4096], P('col', None, 'wide'), may hold values from -6 to 6
- inv_root: float32 [16384, 16384], P('wide', 'col'), as said below
- inv_child: float32 [2, 8192, 8192], P(None, 'wide', 'col'), as said below
- inv_grand: float32 [4, 4096, 4096], P(None, 'wide', 'col'), as said below
- panel_child: float32 [2, 4096, 8192], P(None, 'col', 'wide'), may hold values from -0.046875 to 0.046875
- panel_grand: float32 [4, 2048, 4096], P(None, 'col', 'wide'), may hold values from -0.0625 to 0.0625
- anc_child: int32 [2, 32], P(None, 'col'), may hold values from 0 to 127, as said below
- anc_grand: int32 [4, 16], P(None, 'col'), may hold values from 0 to 255, as said below
Outputs:
- x_root: float32 [512, 16384], P('wide', 'col')
- x_child: float32 [512, 2, 8192], P('wide', None, 'col')
- x_grand: float32 [512, 4, 4096], P('wide', None, 'col')
Inputs may be any that keep to these rules, and one draw needn't show every extreme that they name: inv_root is lower triangular with a positive diagonal (entries above the diagonal are zero). Each inv_child[k] is lower triangular with a positive diagonal. Each inv_grand[g] is lower triangular with a positive diagonal. `anc_child`: each row lists distinct blocks in rising order and always names block 0 and block 127. `anc_grand`: row g lists 2048 // 256 distinct root blocks in rising order, block 0 and block 127 among them, then as many distinct blocks of child g // 2 (numbered 16384 // 128 + (g // 2) * 64 onwards) in rising order, its first and its last among them.
All inputs are finite; a program needn't handle non-finite values.
Results may differ from a plain program's by a relative error of at most 0.000096.
Values sent between devices are 32-bit elements; how exact they have to be, the bound alone decides.
No kernel may reach another device: no remote copies, remote signals or barrier semaphores. Data moves between devices by JAX's collectives and lax.ppermute only.
A program may use at most 128 MiB of HBM per device.

v0:
```python
import jax
import jax.numpy as jnp
from jax import lax
from jax.sharding import PartitionSpec as P

BLK = 128
PRECISE = lax.Precision.HIGHEST


def pick_blocks(source_rows, blocks):
    leading = source_rows.shape[0]
    tiled = source_rows.reshape(leading, source_rows.shape[1] // BLK, BLK)
    selected = jnp.take(tiled, blocks.reshape(-1), axis=1)
    return selected.reshape(leading, blocks.shape[0], blocks.shape[1] * BLK)


def spread_rhs(local_part):
    return lax.all_gather(local_part, "col", axis=0, tiled=True)


def solve_terms(right_rows, inverse):
    return lax.psum_scatter(
        jnp.einsum(
            "ski,kij->skj",
            right_rows,
            inverse,
            precision=PRECISE,
            preferred_element_type=jnp.float32,
        ),
        "wide",
        scatter_dimension=0,
        tiled=True,
    )


def spread_solved(solved_local):
    gathered = lax.all_gather(solved_local, "col", axis=2, tiled=True)
    return gathered.reshape(gathered.shape[0], -1)


def fetch_ancestors(source_rows, blocks):
    return lax.all_gather(pick_blocks(source_rows, blocks), "wide", axis=0, tiled=True)


def finish_level(z_local, inverse, partial_value):
    summed = lax.psum(partial_value, "col")
    right_side = spread_rhs(z_local) - summed
    solved = solve_terms(right_side, inverse)
    return solved


def per_device(
    z_root,
    z_child,
    z_grand,
    inv_root,
    inv_child,
    inv_grand,
    panel_child,
    panel_grand,
    anc_child,
    anc_grand,
):
    root_right = spread_rhs(z_root[:, None, :])
    root_solved = solve_terms(root_right, inv_root[None])
    x_root = root_solved[:, 0, :]
    root_rows = spread_solved(root_solved)
    near_rows = fetch_ancestors(root_rows, anc_child)
    partial_value = jnp.einsum(
        "ska,kaj->skj",
        near_rows,
        panel_child,
        precision=PRECISE,
        preferred_element_type=jnp.float32,
    )
    x_child = finish_level(z_child, inv_child, partial_value)
    child_rows = spread_solved(x_child)
    solved_all = jnp.concatenate([root_rows, child_rows], axis=1)
    far_rows = fetch_ancestors(solved_all, anc_grand)
    partial_grand = jnp.einsum(
        "sga,gaj->sgj", far_rows, panel_grand, precision=PRECISE, preferred_element_type=jnp.float32
    )
    x_grand = finish_level(z_grand, inv_grand, partial_grand)
    return (x_root, x_child, x_grand)


def solution(mesh):
    in_specs = (
        P("col", "wide"),
        P("col", None, "wide"),
        P("col", None, "wide"),
        P("wide", "col"),
        P(None, "wide", "col"),
        P(None, "wide", "col"),
        P(None, "col", "wide"),
        P(None, "col", "wide"),
        P(None, "col"),
        P(None, "col"),
    )
    out_specs = (P("wide", "col"), P("wide", None, "col"), P("wide", None, "col"))
    return jax.shard_map(
        per_device, mesh=mesh, in_specs=in_specs, out_specs=out_specs, check_vma=False
    )
```

profile of v0, /device:TPU:0, one launch (start us, length us, event | category | flops | bytes accessed | tf_op | source)
XLA Modules:
  0.0 726.2 jit_solution(2255232434404925078)
XLA Ops:
  8.0 29.4 %all-gather.21.cloned.1.call-done = f32[512,1024]{1,0:T(8,128)} async-done(((f32[64,1024]{1,0:T(8,128)}), f32[512,1024]{1,0:T(8,128)}) %all-gather.21.cloned.1.call-update) | async-done | bytes 2097168 | tf_op jit(solution)/shard_map/all_gather | solution.py:18
  37.4 30.4 %convolution_bitcast_fusion = f32[512,1,2048]{0,2,1:T(8,128)} fusion(f32[1024,2048]{1,0:T(8,128)} %param.13, f32[512,1024]{1,0:T(8,128)} %all-gather.21.cloned.1.call-done), kind=kOutput, calls=%fused_computation.3 | convolution fusion | flops 12884901888 | bytes 14680064 | tf_op jit(solution)/shard_map/ski,kij->skj/dot_general | solution.py:23
  67.8 11.0 %copy.75 = f32[512,1,2048]{2,1,0:T(1,128)} copy(f32[512,1,2048]{0,2,1:T(8,128)} %convolution_bitcast_fusion) | data formatting | bytes 8388608 | tf_op jit(solution)/shard_map/ski,kij->skj/transpose | solution.py:23
  80.7 102.2 %all-reduce.9.cloned.1.call-done = f32[512,1,2048]{2,1,0:T(1,128)} async-done(((f32[512,1,2048]{2,1,0:T(1,128)}), f32[512,1,2048]{2,1,0:T(1,128)}) %all-reduce.9.cloned.1.call-update) | async-done | bytes 4194320
  183.0 1.7 constant_dynamic-slice_fusion
  184.9 25.1 %all-gather.11.cloned.1.call-done = f32[32,1,16384]{2,1,0:T(1,128)} async-done(((f32[32,1,2048]{2,1,0:T(1,128)}), f32[32,1,16384]{2,1,0:T(1,128)}) %all-gather.11.cloned.1.call-update) | async-done | bytes 2097168 | tf_op jit(solution)/shard_map/all_gather | solution.py:37
  210.0 4.2 copy.77
  214.3 2.1 gather_fusion
  217.3 0.8 copy.76
  218.2 44.9 %all-gather.13.cloned.1.call-done = f32[512,2,512]{2,0,1:T(8,128)} async-done(((f32[32,2,512]{2,0,1:T(8,128)}), f32[512,2,512]{2,0,1:T(8,128)}) %all-gather.13.cloned.1.call-update) | async-done | bytes 2097168 | tf_op jit(solution)/shard_map/all_gather | solution.py:42
  263.0 7.0 convolution_bitcast_fusion.4
  270.1 19.4 %all-gather.9.cloned.1.call-done = f32[512,2,512]{2,0,1:T(8,128)} async-done(((f32[64,2,512]{2,0,1:T(8,128)}), f32[512,2,512]{2,0,1:T(8,128)}) %all-gather.9.cloned.1.call-update) | async-done | bytes 2097168 | tf_op jit(solution)/shard_map/all_gather | solution.py:18
  289.6 68.2 %all-reduce.5.cloned.1.call-done = f32[512,2,512]{2,0,1:T(8,128)} async-done(((f32[512,2,512]{2,0,1:T(8,128)}), f32[512,2,512]{2,0,1:T(8,128)}) %all-reduce.5.cloned.1.call-update) | async-done | bytes 2097168 | tf_op jit(solution)/shard_map/psum | solution.py:46
  357.8 12.2 %convolution_bitcast_fusion.2 = f32[512,2,1024]{2,0,1:T(8,128)} fusion(f32[2,512,1024]{2,1,0:T(8,128)} %param.14, f32[512,2,512]{2,0,1:T(8,128)} %all-gather.9.cloned.1.call-done, f32[512,2,512]{2,0,1:T(8,128)} %all-reduce.5.cloned.1.call-done), kind=kOutput, calls=%fused_computation.5 | convolution fusion | flops 6442975232 | bytes 12582912 | tf_op jit(solution)/shard_map/ski,kij->skj/dot_general | solution.py:23
  370.1 77.5 %reduce-scatter.3.cloned.1.call-done = f32[32,2,1024]{2,0,1:T(8,128)} async-done(((f32[512,2,1024]{2,0,1:T(8,128)}), f32[32,2,1024]{2,0,1:T(8,128)}) %reduce-scatter.3.cloned.1.call-update) | async-done | bytes 262160 | tf_op jit(solution)/shard_map/reduce_scatter | solution.py:22
  447.9 25.8 %all-gather.17.cloned.1.call-done = f32[32,2,8192]{2,0,1:T(8,128)} async-done(((f32[32,2,1024]{2,0,1:T(8,128)}), f32[32,2,8192]{2,0,1:T(8,128)}) %all-gather.17.cloned.1.call-update) | async-done | bytes 2097168 | tf_op jit(solution)/shard_map/all_gather | solution.py:37
  473.7 4.6 copy.81
  478.3 4.0 concatenate.6
  482.3 3.0 copy.83
  485.3 2.4 pad_maximum_fusion
  487.7 2.8 gather_fusion.1
  491.4 1.7 copy.80
  493.2 43.9 %all-gather.19.cloned.1.call-done = f32[512,4,256]{2,0,1:T(8,128)} async-done(((f32[32,4,256]{2,0,1:T(8,128)}), f32[512,4,256]{2,0,1:T(8,128)}) %all-gather.19.cloned.1.call-update) | async-done | bytes 2097168 | tf_op jit(solution)/shard_map/all_gather | solution.py:42
  537.1 4.9 convolution_bitcast_fusion.3
  542.1 21.7 %all-gather.15.cloned.1.call-done = f32[512,4,256]{2,0,1:T(8,128)} async-done(((f32[64,4,256]{2,0,1:T(8,128)}), f32[512,4,256]{2,0,1:T(8,128)}) %all-gather.15.cloned.1.call-update) | async-done | bytes 2097168 | tf_op jit(solution)/shard_map/all_gather | solution.py:18
  563.8 68.5 %all-reduce.7.cloned.1.call-done = f32[512,4,256]{2,0,1:T(8,128)} async-done(((f32[512,4,256]{2,0,1:T(8,128)}), f32[512,4,256]{2,0,1:T(8,128)}) %all-reduce.7.cloned.1.call-update) | async-done | bytes 2097168 | tf_op jit(solution)/shard_map/psum | solution.py:46
  632.3 7.8 %convolution_bitcast_fusion.1 = f32[512,4,512]{2,0,1:T(8,128)} fusion(f32[4,256,512]{2,1,0:T(8,128)S(1)} %copy-done, f32[512,4,256]{2,0,1:T(8,128)} %all-gather.15.cloned.1.call-done, f32[512,4,256]{2,0,1:T(8,128)} %all-reduce.7.cloned.1.call-done), kind=kOutput, calls=%fused_computation.4 | convolution fusion | flops 3221749760 | bytes 10485760 | tf_op jit(solution)/shard_map/ski,kij->skj/dot_general | solution.py:23
  640.0 0.9 copy-done.2
  641.0 0.8 copy.95
  641.8 0.9 copy.87
  642.7 74.9 %reduce-scatter.5.cloned.1.call-done = f32[32,4,512]{2,0,1:T(8,128)} async-done(((f32[512,4,512]{2,0,1:T(8,128)}), f32[32,4,512]{2,0,1:T(8,128)}) %reduce-scatter.5.cloned.1.call-update) | async-done | bytes 262160 | tf_op jit(solution)/shard_map/reduce_scatter | solution.py:22
  717.6 1.8 copy.88
  (60 shorter events, 4.7 us)
Async XLA Ops:
  7.2 625.1 %copy-start = (f32[4,256,512]{2,1,0:T(8,128)S(1)}, f32[4,256,512]{2,1,0:T(8,128)}, u32[]{:S(2)}) copy-start(f32[4,256,512]{2,1,0:T(8,128)} %param.15) | copy-start | bytes 6291460
  7.2 30.2 %all-gather.21.cloned.1.call-start = ((), (), s32[]{:S(2)}) async-start(), calls=%async_computation.12 | async-start | bytes 2359296 | tf_op jit(solution)/shard_map/all_gather | solution.py:18
  7.9 175.0 %all-reduce.9.cloned.1.call-start = ((), (), s32[]{:S(2)}) async-start(), calls=%async_computation.13 | async-start | bytes 8388608
  78.8 0.7 copy-start.8
  78.8 105.9 %copy-start.7 = (s32[2,4]{1,0:T(2,128)S(1)}, s32[2,4]{1,0:T(2,128)}, u32[]{:S(2)}) copy-start(s32[2,4]{1,0:T(2,128)} %param.18) | copy-start | bytes 100
  78.8 131.2 %all-gather.11.cloned.1.call-start = ((), (), s32[]{:S(2)}) async-start(), calls=%async_computation.3 | async-start | bytes 2359296 | tf_op jit(solution)/shard_map/all_gather | solution.py:37
  184.7 78.4 %all-gather.13.cloned.1.call-start = ((), (), s32[]{:S(2)}) async-start(), calls=%async_computation.4 | async-start | bytes 2228224 | tf_op jit(solution)/shard_map/all_gather | solution.py:42
  210.0 7.3 %copy-start.5 = (f32[64,2,512]{2,1,0:T(2,128)S(1)}, f32[64,2,512]{2,1,0:T(2,128)}, u32[]{:S(2)}) copy-start(f32[64,2,512]{2,1,0:T(2,128)} %param.11) | copy-start | bytes 786436
  217.3 72.3 %all-gather.9.cloned.1.call-start = ((), (), s32[]{:S(2)}) async-start(), calls=%async_computation.2 | async-start | bytes 2359296 | tf_op jit(solution)/shard_map/all_gather | solution.py:18
  218.1 139.7 %all-reduce.5.cloned.1.call-start = ((), (), s32[]{:S(2)}) async-start(), calls=%async_computation.5 | async-start | bytes 4194304 | tf_op jit(solution)/shard_map/psum | solution.py:46
  270.1 177.5 %reduce-scatter.3.cloned.1.call-start = ((), (), s32[]{:S(2)}) async-start(), calls=%async_computation.6 | async-start | bytes 4456448 | tf_op jit(solution)/shard_map/reduce_scatter | solution.py:22
  370.0 77.7 %copy-start.6 = (s32[4,2]{0,1:T(2,128)S(1)}, s32[4,2]{0,1:T(2,128)}, u32[]{:S(2)}) copy-start(s32[4,2]{0,1:T(2,128)} %param.19) | copy-start | bytes 100
  370.0 103.7 %all-gather.17.cloned.1.call-start = ((), (), s32[]{:S(2)}) async-start(), calls=%async_computation.8 | async-start | bytes 2359296 | tf_op jit(solution)/shard_map/all_gather | solution.py:37
  447.6 89.6 %all-gather.19.cloned.1.call-start = ((), (), s32[]{:S(2)}) async-start(), calls=%async_computation.9 | async-start | bytes 2228224 | tf_op jit(solution)/shard_map/all_gather | solution.py:42
  482.3 3.0 copy-start.1
  487.7 49.5 %copy-start.3 = (f32[4,256,256]{2,1,0:T(8,128)S(1)}, f32[4,256,256]{2,1,0:T(8,128)}, u32[]{:S(2)}) copy-start(f32[4,256,256]{2,1,0:T(8,128)} %param.17) | copy-start | bytes 3145732
  491.4 72.4 %all-gather.15.cloned.1.call-start = ((), (), s32[]{:S(2)}) async-start(), calls=%async_computation.7 | async-start | bytes 2359296 | tf_op jit(solution)/shard_map/all_gather | solution.py:18
  493.2 139.1 %all-reduce.7.cloned.1.call-start = ((), (), s32[]{:S(2)}) async-start(), calls=%async_computation.10 | async-start | bytes 4194304 | tf_op jit(solution)/shard_map/psum | solution.py:46
  542.0 175.5 %reduce-scatter.5.cloned.1.call-start = ((), (), s32[]{:S(2)}) async-start(), calls=%async_computation.11 | async-start | bytes 4456448 | tf_op jit(solution)/shard_map/reduce_scatter | solution.py:22
  640.0 0.9 copy-start.2
  640.0 1.7 copy-start.4
Sparse Core Ops, SparseCore 0:
  9.7 27.5 all-gather.20
  79.0 103.9 all-reduce.8
  185.2 24.7 all-gather.10
  217.4 45.5 all-gather.12
  265.2 24.3 all-gather.8
  291.8 65.9 all-reduce.4
  370.1 77.3 reduce-scatter.2
  449.4 24.3 all-gather.16
  491.5 45.5 all-gather.18
  539.4 24.3 all-gather.14
  566.3 65.9 all-reduce.6
  640.2 77.3 reduce-scatter.4
where the time goes:
time: 727 us; the launch traced here: 726 us
  waiting for transfers between devices  602 us (83%)
  matrix products  62.3 us (9%)
  local copies, waits for them, and re-layouts  42.2 us (6%)
  between operations  15 us (2%)
    reduce_scatter x2, waiting for transfers between devices, solve_terms(): lax.psum_scatter(jnp.einsum('ski,kij->skj', right_rows, inverse, precisio...  152 us
    psum x2, waiting for transfers between devices, finish_level(): summed = lax.psum(partial_value, 'col')  137 us
    unnamed x13, waiting for transfers between devices  103 us
    all_gather x2, waiting for transfers between devices, fetch_ancestors(): lax.all_gather(pick_blocks(source_rows, blocks), 'wide', axis=0, tiled=True)  88.8 us
    all_gather x3, waiting for transfers between devices, spread_rhs(): return lax.all_gather(local_part, 'col', axis=0, tiled=True)  70.5 us
    all_gather x2, waiting for transfers between devices, spread_solved(): gathered = lax.all_gather(solved_local, 'col', axis=2, tiled=True)  50.9 us
    dot_general x3, matrix products, solve_terms(): jnp.einsum('ski,kij->skj', right_rows, inverse, precision=PRECISE, prefer...  50.4 us
  transfers between devices with their start and end apart: 12, of which 12 were waited for; matrix products, arithmetic and copies ran while one was open for 2% of the time, Pallas kernels for 0%

commit v1 on v0

--- a/solution.py
+++ b/solution.py
@@ -34,7 +34,14 @@
 
 
 def spread_solved(solved_local):
-    gathered = lax.all_gather(solved_local, "col", axis=2, tiled=True)
+    n_dev = lax.axis_size("col")
+    hops = [(i, (i + 1) % n_dev) for i in range(n_dev)]
+    parts = [solved_local]
+    for far in range(1, n_dev):
+        parts = [lax.ppermute(parts[0], "col", hops), *parts]
+    full = jnp.concatenate(parts, axis=2)
+    turn = (lax.axis_index("col") + 1) * parts[-1].shape[2]
+    gathered = jnp.roll(full, turn, axis=2)
     return gathered.reshape(gathered.shape[0], -1)
 
 

time: 727 us -> 779 us (1.072)
  waiting for transfers between devices: 602 us -> 645 us
  local copies, waits for them, and re-layouts: 42.2 us -> 50.5 us
    ppermute x0 -> x14, waiting for transfers between devices: none -> 98.8 us  [spread_solved(): parts = [lax.ppermute(parts[0], 'col', hops), *parts]]
    all_gather x2 -> x0, waiting for transfers between devices: 50.9 us -> none  [spread_solved(): gathered = lax.all_gather(solved_local, 'col', axis=2, tiled=True)]
    unnamed x28 -> x62, local copies, waits for them, and re-layouts: 9.93 us -> 19 us
    unnamed x13 -> x11, waiting for transfers between devices: 103 us -> 103 us
  transfers between devices with their start and end apart: 12 -> 24, of which waited for: 12 -> 24; matrix products, arithmetic and copies ran while one was open for 2% -> 2% of each run, Pallas kernels for 0% -> 0%
where the time goes in v1:
time: 779 us; the launch traced here: 778 us
  waiting for transfers between devices  645 us (83%)
  matrix products  62.4 us (8%)
  local copies, waits for them, and re-layouts  50.5 us (6%)
  between operations  15.2 us (2%)
    reduce_scatter x2, waiting for transfers between devices, solve_terms(): lax.psum_scatter(jnp.einsum('ski,kij->skj', right_rows, inverse, precisio...  154 us
    psum x2, waiting for transfers between devices, finish_level(): summed = lax.psum(partial_value, 'col')  137 us
    unnamed x11, waiting for transfers between devices  103 us
    ppermute x14, waiting for transfers between devices, spread_solved(): parts = [lax.ppermute(parts[0], 'col', hops), *parts]  98.8 us
    all_gather x2, waiting for transfers between devices, fetch_ancestors(): lax.all_gather(pick_blocks(source_rows, blocks), 'wide', axis=0, tiled=True)  82.2 us
    all_gather x3, waiting for transfers between devices, spread_rhs(): return lax.all_gather(local_part, 'col', axis=0, tiled=True)  70.6 us
    dot_general x3, matrix products, solve_terms(): jnp.einsum('ski,kij->skj', right_rows, inverse, precision=PRECISE, prefer...  50.5 us
    unnamed x62, local copies, waits for them, and re-layouts  19 us
  transfers between devices with their start and end apart: 24, of which 24 were waited for; matrix products, arithmetic and copies ran while one was open for 2% of the time, Pallas kernels for 0%

profile of v1, /device:TPU:0, one launch (start us, length us, event | category | flops | bytes accessed | tf_op | source)
XLA Modules:
  0.0 778.0 jit_solution(8227458931803628697)
XLA Ops:
  8.0 29.4 %all-gather.15.cloned.1.call-done = f32[512,1024]{1,0:T(8,128)} async-done(((f32[64,1024]{1,0:T(8,128)}), f32[512,1024]{1,0:T(8,128)}) %all-gather.15.cloned.1.call-update) | async-done | bytes 2097168 | tf_op jit(solution)/shard_map/all_gather | solution.py:18
  37.4 30.5 %convolution_bitcast_fusion = f32[512,1,2048]{0,2,1:T(8,128)} fusion(f32[1024,2048]{1,0:T(8,128)} %param.13, f32[512,1024]{1,0:T(8,128)} %all-gather.15.cloned.1.call-done), kind=kOutput, calls=%fused_computation.3 | convolution fusion | flops 12884901888 | bytes 14680064 | tf_op jit(solution)/shard_map/ski,kij->skj/dot_general | solution.py:23
  67.8 11.0 %copy.53 = f32[512,1,2048]{2,1,0:T(1,128)} copy(f32[512,1,2048]{0,2,1:T(8,128)} %convolution_bitcast_fusion) | data formatting | bytes 8388608 | tf_op jit(solution)/shard_map/ski,kij->skj/transpose | solution.py:23
  80.8 102.3 %all-reduce.9.cloned.1.call-done = f32[512,1,2048]{2,1,0:T(1,128)} async-done(((f32[512,1,2048]{2,1,0:T(1,128)}), f32[512,1,2048]{2,1,0:T(1,128)}) %all-reduce.9.cloned.1.call-update) | async-done | bytes 4194320
  184.1 7.0 collective-permute-done
  191.1 7.0 collective-permute-done.1
  198.1 7.0 collective-permute-done.2
  205.1 7.0 collective-permute-done.3
  212.1 7.1 collective-permute-done.4
  219.6 6.9 collective-permute-done.5
  226.6 7.2 collective-permute-done.6
  245.9 41.8 %all-gather.9.cloned.1.call-done = f32[512,2,512]{2,0,1:T(8,128)} async-done(((f32[32,2,512]{2,0,1:T(8,128)}), f32[512,2,512]{2,0,1:T(8,128)}) %all-gather.9.cloned.1.call-update) | async-done | bytes 2097168 | tf_op jit(solution)/shard_map/all_gather | solution.py:49
  287.7 7.1 convolution_bitcast_fusion.4
  294.8 19.4 %all-gather.7.cloned.1.call-done = f32[512,2,512]{2,0,1:T(8,128)} async-done(((f32[64,2,512]{2,0,1:T(8,128)}), f32[512,2,512]{2,0,1:T(8,128)}) %all-gather.7.cloned.1.call-update) | async-done | bytes 2097168 | tf_op jit(solution)/shard_map/all_gather | solution.py:18
  314.2 68.2 %all-reduce.5.cloned.1.call-done = f32[512,2,512]{2,0,1:T(8,128)} async-done(((f32[512,2,512]{2,0,1:T(8,128)}), f32[512,2,512]{2,0,1:T(8,128)}) %all-reduce.5.cloned.1.call-update) | async-done | bytes 2097168 | tf_op jit(solution)/shard_map/psum | solution.py:53
  382.4 12.2 %convolution_bitcast_fusion.2 = f32[512,2,1024]{2,0,1:T(8,128)} fusion(f32[2,512,1024]{2,1,0:T(8,128)} %param.14, f32[512,2,512]{2,0,1:T(8,128)} %all-gather.7.cloned.1.call-done, f32[512,2,512]{2,0,1:T(8,128)} %all-reduce.5.cloned.1.call-done), kind=kOutput, calls=%fused_computation.5 | convolution fusion | flops 6442975232 | bytes 12582912 | tf_op jit(solution)/shard_map/ski,kij->skj/dot_general | solution.py:23
  394.9 77.3 %reduce-scatter.3.cloned.1.call-done = f32[32,2,1024]{2,0,1:T(8,128)} async-done(((f32[512,2,1024]{2,0,1:T(8,128)}), f32[32,2,1024]{2,0,1:T(8,128)}) %reduce-scatter.3.cloned.1.call-update) | async-done | bytes 262160 | tf_op jit(solution)/shard_map/reduce_scatter | solution.py:22
  472.2 7.2 collective-permute-done.7
  479.4 7.0 collective-permute-done.8
  486.5 7.0 collective-permute-done.9
  493.5 7.0 collective-permute-done.10
  500.5 7.0 collective-permute-done.11
  508.2 7.1 collective-permute-done.12
  515.4 7.2 collective-permute-done.13
  528.9 3.0 copy.62
  531.9 4.0 concatenate.20
  548.3 40.4 %all-gather.13.cloned.1.call-done = f32[512,4,256]{2,0,1:T(8,128)} async-done(((f32[32,4,256]{2,0,1:T(8,128)}), f32[512,4,256]{2,0,1:T(8,128)}) %all-gather.13.cloned.1.call-update) | async-done | bytes 2097168 | tf_op jit(solution)/shard_map/all_gather | solution.py:49
  588.8 4.9 convolution_bitcast_fusion.3
  593.7 21.8 %all-gather.11.cloned.1.call-done = f32[512,4,256]{2,0,1:T(8,128)} async-done(((f32[64,4,256]{2,0,1:T(8,128)}), f32[512,4,256]{2,0,1:T(8,128)}) %all-gather.11.cloned.1.call-update) | async-done | bytes 2097168 | tf_op jit(solution)/shard_map/all_gather | solution.py:18
  615.5 68.5 %all-reduce.7.cloned.1.call-done = f32[512,4,256]{2,0,1:T(8,128)} async-done(((f32[512,4,256]{2,0,1:T(8,128)}), f32[512,4,256]{2,0,1:T(8,128)}) %all-reduce.7.cloned.1.call-update) | async-done | bytes 2097168 | tf_op jit(solution)/shard_map/psum | solution.py:53
  684.0 7.8 convolution_bitcast_fusion.1
  692.7 76.6 %reduce-scatter.5.cloned.1.call-done = f32[32,4,512]{2,0,1:T(8,128)} async-done(((f32[512,4,512]{2,0,1:T(8,128)}), f32[32,4,512]{2,0,1:T(8,128)}) %reduce-scatter.5.cloned.1.call-update) | async-done | bytes 262160 | tf_op jit(solution)/shard_map/reduce_scatter | solution.py:22
  (118 shorter events, 37.8 us)
Async XLA Ops:
  7.2 676.9 %copy-start = (f32[4,256,512]{2,1,0:T(8,128)S(1)}, f32[4,256,512]{2,1,0:T(8,128)}, u32[]{:S(2)}) copy-start(f32[4,256,512]{2,1,0:T(8,128)} %param.15) | copy-start | bytes 6291460
  7.2 30.2 %all-gather.15.cloned.1.call-start = ((), (), s32[]{:S(2)}) async-start(), calls=%async_computation.10 | async-start | bytes 2359296 | tf_op jit(solution)/shard_map/all_gather | solution.py:18
  7.9 175.1 %all-reduce.9.cloned.1.call-start = ((), (), s32[]{:S(2)}) async-start(), calls=%async_computation.11 | async-start | bytes 8388608
  78.9 140.4 %copy-start.8 = (s32[2,4]{1,0:T(2,128)S(1)}, s32[2,4]{1,0:T(2,128)}, u32[]{:S(2)}) copy-start(s32[2,4]{1,0:T(2,128)} %param.18) | copy-start | bytes 100
  78.9 140.5 %copy-start.7 = (s32[4,2]{0,1:T(2,128)S(1)}, s32[4,2]{0,1:T(2,128)}, u32[]{:S(2)}) copy-start(s32[4,2]{0,1:T(2,128)} %param.19) | copy-start | bytes 100
  78.9 208.8 %all-gather.9.cloned.1.call-start = ((), (), s32[]{:S(2)}) async-start(), calls=%async_computation.3 | async-start | bytes 2228224 | tf_op jit(solution)/shard_map/all_gather | solution.py:49
  184.1 7.0 collective-permute-start
  191.1 7.0 collective-permute-start.1
  198.1 7.0 collective-permute-start.2
  205.1 7.0 collective-permute-start.3
  212.1 7.1 collective-permute-start.4
  219.2 7.3 collective-permute-start.5
  226.6 7.2 collective-permute-start.6
  239.0 6.1 copy-start.6
  245.0 69.2 %all-gather.7.cloned.1.call-start = ((), (), s32[]{:S(2)}) async-start(), calls=%async_computation.2 | async-start | bytes 2359296 | tf_op jit(solution)/shard_map/all_gather | solution.py:18
  245.8 136.5 %all-reduce.5.cloned.1.call-start = ((), (), s32[]{:S(2)}) async-start(), calls=%async_computation.4 | async-start | bytes 4194304 | tf_op jit(solution)/shard_map/psum | solution.py:53
  294.8 177.5 %reduce-scatter.3.cloned.1.call-start = ((), (), s32[]{:S(2)}) async-start(), calls=%async_computation.5 | async-start | bytes 4456448 | tf_op jit(solution)/shard_map/reduce_scatter | solution.py:22
  394.6 194.1 %all-gather.13.cloned.1.call-start = ((), (), s32[]{:S(2)}) async-start(), calls=%async_computation.7 | async-start | bytes 2228224 | tf_op jit(solution)/shard_map/all_gather | solution.py:49
  472.2 56.5 %copy-start.2 = (f32[32,2,1024]{2,0,1:T(8,128)S(1)}, f32[32,2,1024]{2,0,1:T(8,128)}, u32[]{:S(2)}) copy-start(f32[32,2,1024]{2,0,1:T(8,128)} %reduce-scatter.3.cloned.1.call-done) | copy-start | bytes 786436
  472.2 7.2 collective-permute-start.7
  479.4 7.0 collective-permute-start.8
  486.5 7.0 collective-permute-start.9
  493.5 7.0 collective-permute-start.10
  500.5 7.0 collective-permute-start.11
  508.2 7.1 collective-permute-start.12
  515.3 7.3 collective-permute-start.13
  515.3 13.2 %copy-start.5 = (f32[32,2,1024]{2,0,1:T(8,128)S(1)}, f32[32,2,1024]{2,0,1:T(8,128)}, u32[]{:S(2)}) copy-start(f32[32,2,1024]{2,0,1:T(8,128)} %copy-done.4) | copy-start | bytes 786436
  535.9 3.0 copy-start.1
  538.9 49.9 %copy-start.3 = (f32[4,256,256]{2,1,0:T(8,128)S(1)}, f32[4,256,256]{2,1,0:T(8,128)}, u32[]{:S(2)}) copy-start(f32[4,256,256]{2,1,0:T(8,128)} %param.17) | copy-start | bytes 3145732
  546.5 69.0 %all-gather.11.cloned.1.call-start = ((), (), s32[]{:S(2)}) async-start(), calls=%async_computation.6 | async-start | bytes 2359296 | tf_op jit(solution)/shard_map/all_gather | solution.py:18
  548.3 135.7 %all-reduce.7.cloned.1.call-start = ((), (), s32[]{:S(2)}) async-start(), calls=%async_computation.8 | async-start | bytes 4194304 | tf_op jit(solution)/shard_map/psum | solution.py:53
  593.7 175.6 %reduce-scatter.5.cloned.1.call-start = ((), (), s32[]{:S(2)}) async-start(), calls=%async_computation.9 | async-start | bytes 4456448 | tf_op jit(solution)/shard_map/reduce_scatter | solution.py:22
  (2 other events, 1.4 us)
Sparse Core Ops, SparseCore 0:
  9.7 27.5 all-gather.14
  79.0 103.9 all-reduce.8
  245.1 42.5 all-gather.8
  289.8 24.3 all-gather.6
  316.4 65.9 all-reduce.4
  394.8 77.4 reduce-scatter.2
  546.6 42.0 all-gather.12
  591.1 24.3 all-gather.10
  618.0 65.9 all-reduce.6
  691.9 77.3 reduce-scatter.4
